TPU v7x, 512 devices: a whole 4x8x8 slice. The times are simulated.
512 devices in a mesh: dp: 16 (over z, core), ctx: 32 (over y, x).
Axes of the slice: x: 4, y: 8, z: 8, core: 2. Of those that a mesh axis runs over, the one named last changes fastest.
Arguments:
- positions: int32 [49152], P('dp'), parts along dimension 0, may hold values from 0 to 24575, as said below
- queries: bfloat16 [147456, 2048], P(('dp', 'ctx')), parts along dimension 0, may hold values from -12 to 12
- keys_values: bfloat16 [147456, 1024], P(('dp', 'ctx')), parts along dimension 0, may hold values from -12 to 12
- router_weight: bfloat16 [147456], P(('dp', 'ctx')), parts along dimension 0, may hold values from 0.25 to 2
Outputs:
- attended: bfloat16 [147456, 2048], P(('dp', 'ctx')), parts along dimension 0
There are 16 independent parts, one for each index of `dp`. A program takes and returns all parts, laid end to end along the dimension named above; each array names one. Nothing has to cross between parts.
Inputs may be any that keep to these rules, and one draw needn't show every extreme that they name: Distinct and increasing. The shard of positions d * 768 to (d + 1) * 768 - 1 holds at most 288 of them, and one shard holds exactly 288; slots of device d's blocks beyond counts[d] hold data that no output reads.
All inputs are finite; a program needn't handle non-finite values.
Results may differ from a plain program's by a relative error of at most 0.0085.
Values may be sent and summed in bfloat16 or wider, within the bound.
No kernel may reach another device: no remote copies, remote signals or barrier semaphores. Data moves between devices by JAX's collectives and lax.ppermute only.
A program may use at most 64 MiB of HBM per device.

v0:
```python
import math
import jax
import jax.numpy as jnp
from jax import lax
from jax.sharding import PartitionSpec as P

QUERY_HEADS = 16
KEY_VALUE_HEADS = 4
HEAD_SIZE = 128
SEL_DEV = 96
TOK_DEV = 768
CAP = 288
large_negative_fill = -1e30


def shard_offsets(positions, devices_ctx):
    bounds = jnp.arange(devices_ctx + 1, dtype=jnp.int32) * TOK_DEV
    return jnp.sum((positions[None, :] < bounds[:, None]).astype(jnp.int32), axis=1)


def pack_forward(arrays, offsets, my_rank, devices_ctx, pair_slots):
    my_start = offsets[my_rank]
    my_count = offsets[my_rank + 1] - my_start
    target = jnp.arange(devices_ctx, dtype=jnp.int32)[:, None]
    slot_index = jnp.arange(pair_slots, dtype=jnp.int32)[None, :]
    global_idx = (my_start // devices_ctx + slot_index) * devices_ctx + target
    local_idx = global_idx - my_start
    usable = ((local_idx >= 0) & (local_idx < my_count)).reshape(-1)
    picked = jnp.clip(local_idx, 0, CAP - 1).reshape(-1)
    result = []
    for member in arrays:
        gathered_rows = jnp.take(member, picked, axis=0)
        mask_shape = usable.reshape(usable.shape + (1,) * (gathered_rows.ndim - 1))
        gathered_rows = jnp.where(mask_shape, gathered_rows, jnp.zeros_like(gathered_rows))
        result.append(gathered_rows.reshape((devices_ctx, pair_slots) + member.shape[1:]))
    return tuple(result)


def unpack_forward(received, offsets, my_rank, devices_ctx, pair_slots):
    slot_ids = jnp.arange(SEL_DEV, dtype=jnp.int32)
    global_idx = slot_ids * devices_ctx + my_rank
    owners = jnp.sum((offsets[None, 1:] <= global_idx[:, None]).astype(jnp.int32), axis=1)
    slot_index = slot_ids - jnp.take(offsets, owners) // devices_ctx
    picked = owners * pair_slots + slot_index
    return tuple(
        (jnp.take(member.reshape((-1,) + member.shape[2:]), picked, axis=0) for member in received)
    )


def pack_return(scaled, offsets, my_rank, devices_ctx, pair_slots):
    starts = offsets[:-1][:, None]
    ends = offsets[1:][:, None]
    slot_index = jnp.arange(pair_slots, dtype=jnp.int32)[None, :]
    local_idx = starts // devices_ctx + slot_index
    global_idx = local_idx * devices_ctx + my_rank
    usable = ((local_idx < SEL_DEV) & (global_idx >= starts) & (global_idx < ends)).reshape(-1)
    picked = jnp.clip(local_idx, 0, SEL_DEV - 1).reshape(-1)
    gathered_rows = jnp.take(scaled, picked, axis=0)
    gathered_rows = jnp.where(usable[:, None], gathered_rows, jnp.zeros_like(gathered_rows))
    return gathered_rows.reshape(devices_ctx, pair_slots, scaled.shape[1])


def unpack_return(received, offsets, my_rank, devices_ctx, pair_slots):
    my_start = offsets[my_rank]
    my_count = offsets[my_rank + 1] - my_start
    slot_ids = jnp.arange(CAP, dtype=jnp.int32)
    global_idx = my_start + slot_ids
    live_slot = slot_ids < my_count
    source = global_idx % devices_ctx
    slot_index = jnp.clip(global_idx // devices_ctx - my_start // devices_ctx, 0, pair_slots - 1)
    flat = received.reshape(-1, received.shape[2])
    gathered_rows = jnp.take(flat, source * pair_slots + slot_index, axis=0)
    return jnp.where(live_slot[:, None], gathered_rows, jnp.zeros_like(gathered_rows))


def block_divisions(rows_total):
    for num_blocks in range(1, rows_total + 1):
        if rows_total % num_blocks == 0 and rows_total // num_blocks <= 512:
            return num_blocks
    return rows_total


def attend(query_row_count, query_index, kv_bal, devices_ctx):
    query_row_total = query_row_count.shape[0]
    group_count = QUERY_HEADS // KEY_VALUE_HEADS
    grouped_heads = query_row_count.reshape(
        query_row_total, KEY_VALUE_HEADS, group_count, HEAD_SIZE
    )
    score_scale = 1.0 / math.sqrt(HEAD_SIZE)

    def update(running, key_block_start, block_start):
        max_run, total_run, accum = running
        key_total_count = key_block_start.shape[0]
        key_rows = block_start + jnp.arange(key_total_count, dtype=jnp.int32)
        key_index = key_rows % SEL_DEV * devices_ctx + key_rows // SEL_DEV
        block_key_rows = key_block_start[:, : KEY_VALUE_HEADS * HEAD_SIZE].reshape(
            key_total_count, KEY_VALUE_HEADS, HEAD_SIZE
        )
        block_value_rows = key_block_start[:, KEY_VALUE_HEADS * HEAD_SIZE :].reshape(
            key_total_count, KEY_VALUE_HEADS, HEAD_SIZE
        )
        scores = (
            jnp.einsum(
                "qkgd,ckd->kgqc", grouped_heads, block_key_rows, preferred_element_type=jnp.float32
            )
            * score_scale
        )
        visible = key_index[None, :] <= query_index[:, None]
        scores = jnp.where(visible, scores, large_negative_fill)
        max_new = jnp.maximum(max_run, jnp.max(scores, axis=-1))
        weights = jnp.where(visible, jnp.exp(scores - max_new[..., None]), 0.0)
        factor = jnp.exp(max_run - max_new)
        total_new = total_run * factor + jnp.sum(weights, axis=-1)
        weighted = jnp.einsum(
            "kgqc,ckd->qkgd",
            weights.astype(jnp.bfloat16),
            block_value_rows,
            preferred_element_type=jnp.float32,
        )
        accum_new = accum * jnp.transpose(factor, (2, 0, 1))[..., None] + weighted
        return (max_new, total_new, accum_new)

    def fold_piece(running, piece_rows, piece_start):
        num_blocks = block_divisions(piece_rows.shape[0])
        if num_blocks == 1:
            return update(running, piece_rows, piece_start)
        block_rows = piece_rows.shape[0] // num_blocks
        blocks = piece_rows.reshape(num_blocks, block_rows, piece_rows.shape[1])

        def scan_step(running_in, inputs_in):
            key_block_start, order_id = inputs_in
            return (update(running_in, key_block_start, piece_start + order_id * block_rows), None)

        running_out, unused = lax.scan(
            scan_step, running, (blocks, jnp.arange(num_blocks, dtype=jnp.int32))
        )
        return running_out

    initial = (
        jnp.full((KEY_VALUE_HEADS, group_count, query_row_total), large_negative_fill, jnp.float32),
        jnp.zeros((KEY_VALUE_HEADS, group_count, query_row_total), jnp.float32),
        jnp.zeros((query_row_total, KEY_VALUE_HEADS, group_count, HEAD_SIZE), jnp.float32),
    )
    max_run, total_run, accum = fold_piece(
        initial, lax.all_gather(kv_bal, "ctx", axis=0, tiled=True), jnp.int32(0)
    )
    result = accum / jnp.transpose(total_run, (2, 0, 1))[..., None]
    return result.reshape(query_row_total, QUERY_HEADS * HEAD_SIZE)


def per_device(positions, queries, keys_values, router_weight):
    devices_ctx = lax.axis_size("ctx")
    my_rank = lax.axis_index("ctx")
    pair_slots = (CAP + devices_ctx - 1) // devices_ctx + 1
    offsets = shard_offsets(positions, devices_ctx)
    packed = pack_forward(
        (queries, keys_values, router_weight), offsets, my_rank, devices_ctx, pair_slots
    )
    moved = (
        lax.all_to_all(packed[0], "ctx", split_axis=0, concat_axis=0, tiled=True),
        lax.all_to_all(packed[1], "ctx", split_axis=0, concat_axis=0, tiled=True),
        lax.all_to_all(packed[2], "ctx", split_axis=0, concat_axis=0, tiled=True),
    )
    query_bal, kv_bal, gate_bal = unpack_forward(moved, offsets, my_rank, devices_ctx, pair_slots)
    query_index = jnp.arange(SEL_DEV, dtype=jnp.int32) * devices_ctx + my_rank
    attended = attend(query_bal, query_index, kv_bal, devices_ctx)
    scaled = (gate_bal.astype(jnp.float32)[:, None] * attended).astype(jnp.bfloat16)
    outgoing = pack_return(scaled, offsets, my_rank, devices_ctx, pair_slots)
    returned = lax.all_to_all(outgoing, "ctx", split_axis=0, concat_axis=0, tiled=True)
    return unpack_return(returned, offsets, my_rank, devices_ctx, pair_slots)


def solution(mesh):
    in_specs = (P("dp"), P(("dp", "ctx"), None), P(("dp", "ctx"), None), P(("dp", "ctx")))
    out_specs = P(("dp", "ctx"), None)
    return jax.shard_map(
        per_device, mesh=mesh, in_specs=in_specs, out_specs=out_specs, check_vma=False
    )
```

profile of v0, /device:TPU:16, one launch (start us, length us, event | category | flops | bytes accessed | tf_op | source)
XLA Modules:
  0.0 319.8 jit_solution(5905198751178517340)
XLA Ops:
  12.8 3.6 %gather_fusion.1 = bf16[320]{0:T(512)(128)(2,1)S(1)} fusion(bf16[288]{0:T(512)(128)(2,1)} %param.9, s32[1024]{0:T(1024)S(1)} %pad_clamp_fusion.3), kind=kCustom, calls=%fused_computation.1 | custom fusion | bytes 2560 | tf_op jit(solution)/shard_map/jit(_take)/gather | solution.py:32
  17.8 10.1 %all-to-all-start = ((bf16[32,1,10]{2,1,0:T(2,128)(2,1)}), bf16[32,1,10]{2,1,0:T(2,128)(2,1)S(1)}, u32[]{:S(2)}, u32[]{:S(2)}) async-start(bf16[32,1,10]{2,1,0:T(2,128)(2,1)} %copy.20), calls=%async_computation | async-start | bytes 32768 | tf_op jit(solution)/shard_map/all_to_all | solution.py:162
  32.1 3.6 %all-to-all-done = bf16[32,1,10]{2,1,0:T(2,128)(2,1)S(1)} async-done(((bf16[32,1,10]{2,1,0:T(2,128)(2,1)}), bf16[32,1,10]{2,1,0:T(2,128)(2,1)S(1)}, u32[]{:S(2)}, u32[]{:S(2)}) %all-to-all-start) | async-done | bytes 672 | tf_op jit(solution)/shard_map/all_to_all | solution.py:162
  35.6 6.2 %all-to-all-start.1 = ((bf16[32,10,1024]{2,1,0:T(8,128)(2,1)}), bf16[32,10,1024]{2,1,0:T(8,128)(2,1)S(1)}, u32[]{:S(2)}, u32[]{:S(2)}) async-start(bf16[32,10,1024]{2,1,0:T(8,128)(2,1)} %select_select_fusion.3), calls=%async_computation.1 | async-start | bytes 2097152 | tf_op jit(solution)/shard_map/all_to_all | solution.py:161
  44.8 24.6 %all-to-all-done.1 = bf16[32,10,1024]{2,1,0:T(8,128)(2,1)S(1)} async-done(((bf16[32,10,1024]{2,1,0:T(8,128)(2,1)}), bf16[32,10,1024]{2,1,0:T(8,128)(2,1)S(1)}, u32[]{:S(2)}, u32[]{:S(2)}) %all-to-all-start.1) | async-done | bytes 655392 | tf_op jit(solution)/shard_map/all_to_all | solution.py:161
  71.3 3.0 gather_fusion.5
  78.3 5.5 %all-to-all-start.2 = ((bf16[32,10,2048]{2,1,0:T(8,128)(2,1)}), bf16[32,10,2048]{2,1,0:T(8,128)(2,1)}, u32[]{:S(2)}, u32[]{:S(2)}) async-start(bf16[32,10,2048]{2,1,0:T(8,128)(2,1)} %select_select_fusion.1), calls=%async_computation.2 | async-start | bytes 4194304 | tf_op jit(solution)/shard_map/all_to_all | solution.py:160
  84.2 56.0 %all-to-all-done.2 = bf16[32,10,2048]{2,1,0:T(8,128)(2,1)} async-done(((bf16[32,10,2048]{2,1,0:T(8,128)(2,1)}), bf16[32,10,2048]{2,1,0:T(8,128)(2,1)}, u32[]{:S(2)}, u32[]{:S(2)}) %all-to-all-start.2) | async-done | bytes 1310752 | tf_op jit(solution)/shard_map/all_to_all | solution.py:160
  140.2 2.5 reshape.582
  144.6 30.1 %all-gather.2.cloned.1.call-done = bf16[3072,1024]{1,0:T(8,128)(2,1)} async-done(((bf16[96,1024]{1,0:T(8,128)(2,1)}), bf16[3072,1024]{1,0:T(8,128)(2,1)}) %all-gather.2.cloned.1.call-update) | async-done | bytes 6291472 | tf_op jit(solution)/shard_map/all_gather | solution.py:145
  174.7 64.7 %while.17 = (s32[]{:T(128)}, f32[4,4,96]{2,1,0:T(4,128)S(1)}, f32[4,4,96]{2,1,0:T(4,128)S(1)}, f32[96,4,4,128]{3,0,2,1:T(8,128)}, s32[6]{0:T(128)S(1)}, /*index=...) while((s32[]{:T(128)}, f32[4,4,96]{2,1,0:T(4,128)S(1)}, ...), condition=%wide.region_5.6_spmd.clone, body=%wide.region_2.5_spmd.clone.sunk | while | flops 413532864 | bytes 39490572 | solution.py:134
  181.4 2.9 fusion.85
  189.9 2.3 fusion.81
  192.2 2.9 fusion.85
  203.0 2.9 fusion.85
  213.8 2.9 fusion.85
  224.6 2.9 fusion.85
  235.3 2.9 fusion.85
  241.8 3.0 gather_fusion.7
  248.8 6.3 %all-to-all-start.3 = ((bf16[32,10,2048]{2,1,0:T(8,128)(2,1)}), bf16[32,10,2048]{2,1,0:T(8,128)(2,1)}, u32[]{:S(2)}, u32[]{:S(2)}) async-start(bf16[32,10,2048]{2,1,0:T(8,128)(2,1)} %select_select_fusion), calls=%async_computation.3 | async-start | bytes 4194304 | tf_op jit(solution)/shard_map/all_to_all | solution.py:169
  256.4 48.6 %all-to-all-done.3 = bf16[32,10,2048]{2,1,0:T(8,128)(2,1)} async-done(((bf16[32,10,2048]{2,1,0:T(8,128)(2,1)}), bf16[32,10,2048]{2,1,0:T(8,128)(2,1)}, u32[]{:S(2)}, u32[]{:S(2)}) %all-to-all-start.3) | async-done | bytes 1310752 | tf_op jit(solution)/shard_map/all_to_all | solution.py:169
  305.0 2.5 reshape.584
  307.5 3.0 gather_fusion.8
  310.5 2.5 select_select_fusion.2
  (179 shorter events, 66.5 us)
Async XLA Ops:
  6.5 64.7 %copy-start = (bf16[288,2048]{1,0:T(8,128)(2,1)S(1)}, bf16[288,2048]{1,0:T(8,128)(2,1)}, u32[]{:S(2)}) copy-start(bf16[288,2048]{1,0:T(8,128)(2,1)} %param.7) | copy-start | bytes 3538948
  6.5 22.0 %copy-start.2 = (bf16[288,1024]{1,0:T(8,128)(2,1)S(1)}, bf16[288,1024]{1,0:T(8,128)(2,1)}, u32[]{:S(2)}) copy-start(bf16[288,1024]{1,0:T(8,128)(2,1)} %param.8) | copy-start | bytes 1769476
  17.8 17.8 %all-to-all-start = ((bf16[32,1,10]{2,1,0:T(2,128)(2,1)}), bf16[32,1,10]{2,1,0:T(2,128)(2,1)S(1)}, u32[]{:S(2)}, u32[]{:S(2)}) async-start(bf16[32,1,10]{2,1,0:T(2,128)(2,1)} %copy.20), calls=%async_computation | async-start | bytes 32768 | tf_op jit(solution)/shard_map/all_to_all | solution.py:162
  35.6 33.8 %all-to-all-start.1 = ((bf16[32,10,1024]{2,1,0:T(8,128)(2,1)}), bf16[32,10,1024]{2,1,0:T(8,128)(2,1)S(1)}, u32[]{:S(2)}, u32[]{:S(2)}) async-start(bf16[32,10,1024]{2,1,0:T(8,128)(2,1)} %select_select_fusion.3), calls=%async_computation.1 | async-start | bytes 2097152 | tf_op jit(solution)/shard_map/all_to_all | solution.py:161
  41.8 132.9 %all-gather.2.cloned.1.call-start = ((), (), s32[]{:S(2)}) async-start(), calls=%async_computation.4 | async-start | bytes 6488064 | tf_op jit(solution)/shard_map/all_gather | solution.py:145
  78.3 61.9 %all-to-all-start.2 = ((bf16[32,10,2048]{2,1,0:T(8,128)(2,1)}), bf16[32,10,2048]{2,1,0:T(8,128)(2,1)}, u32[]{:S(2)}, u32[]{:S(2)}) async-start(bf16[32,10,2048]{2,1,0:T(8,128)(2,1)} %select_select_fusion.1), calls=%async_computation.2 | async-start | bytes 4194304 | tf_op jit(solution)/shard_map/all_to_all | solution.py:160
  178.2 3.2 %copy-start.4 = (f32[96,4,4,128]{3,0,2,1:T(8,128)S(1)}, f32[96,4,4,128]{3,0,2,1:T(8,128)}, u32[]{:S(2)}) copy-start(f32[96,4,4,128]{3,0,2,1:T(8,128)} %get-tuple-element.274) | copy-start | bytes 2359300 | tf_op jit(solution)/shard_map/while
  181.4 2.9 copy-start.1
  184.3 1.1 copy-start.5
  188.9 3.2 %copy-start.4 = (f32[96,4,4,128]{3,0,2,1:T(8,128)S(1)}, f32[96,4,4,128]{3,0,2,1:T(8,128)}, u32[]{:S(2)}) copy-start(f32[96,4,4,128]{3,0,2,1:T(8,128)} %get-tuple-element.274) | copy-start | bytes 2359300 | tf_op jit(solution)/shard_map/while
  192.2 2.9 copy-start.1
  195.1 1.1 copy-start.5
  199.7 3.2 %copy-start.4 = (f32[96,4,4,128]{3,0,2,1:T(8,128)S(1)}, f32[96,4,4,128]{3,0,2,1:T(8,128)}, u32[]{:S(2)}) copy-start(f32[96,4,4,128]{3,0,2,1:T(8,128)} %get-tuple-element.274) | copy-start | bytes 2359300 | tf_op jit(solution)/shard_map/while
  203.0 2.9 copy-start.1
  205.9 1.1 copy-start.5
  210.5 3.2 %copy-start.4 = (f32[96,4,4,128]{3,0,2,1:T(8,128)S(1)}, f32[96,4,4,128]{3,0,2,1:T(8,128)}, u32[]{:S(2)}) copy-start(f32[96,4,4,128]{3,0,2,1:T(8,128)} %get-tuple-element.274) | copy-start | bytes 2359300 | tf_op jit(solution)/shard_map/while
  213.8 2.9 copy-start.1
  221.3 3.2 %copy-start.4 = (f32[96,4,4,128]{3,0,2,1:T(8,128)S(1)}, f32[96,4,4,128]{3,0,2,1:T(8,128)}, u32[]{:S(2)}) copy-start(f32[96,4,4,128]{3,0,2,1:T(8,128)} %get-tuple-element.274) | copy-start | bytes 2359300 | tf_op jit(solution)/shard_map/while
  224.5 2.9 copy-start.1
  227.5 1.1 copy-start.5
  232.1 3.2 %copy-start.4 = (f32[96,4,4,128]{3,0,2,1:T(8,128)S(1)}, f32[96,4,4,128]{3,0,2,1:T(8,128)}, u32[]{:S(2)}) copy-start(f32[96,4,4,128]{3,0,2,1:T(8,128)} %get-tuple-element.274) | copy-start | bytes 2359300 | tf_op jit(solution)/shard_map/while
  235.3 2.9 copy-start.1
  238.3 1.1 copy-start.5
  248.8 56.2 %all-to-all-start.3 = ((bf16[32,10,2048]{2,1,0:T(8,128)(2,1)}), bf16[32,10,2048]{2,1,0:T(8,128)(2,1)}, u32[]{:S(2)}, u32[]{:S(2)}) async-start(bf16[32,10,2048]{2,1,0:T(8,128)(2,1)} %select_select_fusion), calls=%async_computation.3 | async-start | bytes 4194304 | tf_op jit(solution)/shard_map/all_to_all | solution.py:169
  (7 other events, 7.1 us)
Sparse Core Ops, SparseCore 0:
  71.4 103.2 all-gather.1
where the time goes:
time: 321 us; the launch traced here: 320 us
  waiting for transfers between devices  163 us (51%)
  local copies, waits for them, and re-layouts  52.7 us (16%)
  matrix products  31.3 us (10%)
  starting transfers between devices  28.1 us (9%)
  other arithmetic  22.4 us (7%)
  between operations  17.5 us (5%)
  loops' own time  4.95 us (2%)
    all_to_all x1, waiting for transfers between devices, per_device(): lax.all_to_all(packed[0], 'ctx', split_axis=0, concat_axis=0, tiled=True)  56 us
    all_to_all x1, waiting for transfers between devices, per_device(): lax.all_to_all(outgoing, 'ctx', split_axis=0, concat_axis=0, tiled=True)  48.6 us
    all_gather x1, waiting for transfers between devices, attend(): lax.all_gather(kv_bal, 'ctx', axis=0, tiled=True)  30.1 us
    all_to_all x1, waiting for transfers between devices, per_device(): lax.all_to_all(packed[1], 'ctx', split_axis=0, concat_axis=0, tiled=True)  24.6 us
    dot_general x6, matrix products, update(): jnp.einsum('kgqc,ckd->qkgd', weights.astype(jnp.bfloat16), block_value_ro...  17.5 us
    dynamic_slice x18, local copies, waits for them, and re-layouts, fold_piece(): lax.scan(scan_step, running, (blocks, jnp.arange(num_blocks, dtype=jnp.in...  15 us
    dot_general x6, matrix products, update(): jnp.einsum('qkgd,ckd->kgqc', grouped_heads, block_key_rows, preferred_ele...  13.9 us
    gather x6, local copies, waits for them, and re-layouts, pack_forward(): gathered_rows = jnp.take(member, picked, axis=0)  11.4 us
  transfers between devices with their start and end apart: 5, of which 5 were waited for; matrix products, arithmetic and copies ran while one was open for 6% of the time, Pallas kernels for 0%

commit v1 on v0

--- a/solution.py
+++ b/solution.py
@@ -11,6 +11,13 @@
 TOK_DEV = 768
 CAP = 288
 large_negative_fill = -1e30
+
+
+def enter_windows(here_x, named_axis):
+    main = jnp.stack([here_x for _ in range(lax.axis_size(named_axis))])
+    return jnp.concatenate(
+        lax.all_to_all(main, axis_name=named_axis, split_axis=0, concat_axis=0), axis=0
+    )
 
 
 def shard_offsets(positions, devices_ctx):
@@ -141,9 +148,7 @@
         jnp.zeros((KEY_VALUE_HEADS, group_count, query_row_total), jnp.float32),
         jnp.zeros((query_row_total, KEY_VALUE_HEADS, group_count, HEAD_SIZE), jnp.float32),
     )
-    max_run, total_run, accum = fold_piece(
-        initial, lax.all_gather(kv_bal, "ctx", axis=0, tiled=True), jnp.int32(0)
-    )
+    max_run, total_run, accum = fold_piece(initial, enter_windows(kv_bal, "ctx"), jnp.int32(0))
     result = accum / jnp.transpose(total_run, (2, 0, 1))[..., None]
     return result.reshape(query_row_total, QUERY_HEADS * HEAD_SIZE)
 

time: 321 us -> 404 us (1.26)
  the two profiles are of different devices: /device:TPU:16 before, /device:TPU:2 now
where the time goes in v1:
time: 404 us; the launch traced here: 403 us
  waiting for transfers between devices  248 us (61%)
  local copies, waits for them, and re-layouts  59.7 us (15%)
  starting transfers between devices  32.4 us (8%)
  matrix products  31.3 us (8%)
  other arithmetic  23 us (6%)
  loops' own time  4.61 us (1%)
  between operations  4.45 us (1%)
    all_to_all x1, waiting for transfers between devices, enter_windows(): lax.all_to_all(main, axis_name=named_axis, split_axis=0, concat_axis=0)  135 us
    all_to_all x1, waiting for transfers between devices, per_device(): lax.all_to_all(outgoing, 'ctx', split_axis=0, concat_axis=0, tiled=True)  48.1 us
    all_to_all x1, waiting for transfers between devices, per_device(): lax.all_to_all(packed[0], 'ctx', split_axis=0, concat_axis=0, tiled=True)  39.7 us
    all_to_all x1, waiting for transfers between devices, per_device(): lax.all_to_all(packed[1], 'ctx', split_axis=0, concat_axis=0, tiled=True)  20.5 us
    dot_general x6, matrix products, update(): jnp.einsum('kgqc,ckd->qkgd', weights.astype(jnp.bfloat16), block_value_ro...  17.5 us
    dynamic_slice x18, local copies, waits for them, and re-layouts, fold_piece(): lax.scan(scan_step, running, (blocks, jnp.arange(num_blocks, dtype=jnp.in...  14.7 us
    dot_general x6, matrix products, update(): jnp.einsum('qkgd,ckd->kgqc', grouped_heads, block_key_rows, preferred_ele...  13.9 us
    gather x6, local copies, waits for them, and re-layouts, pack_forward(): gathered_rows = jnp.take(member, picked, axis=0)  11.4 us
  transfers between devices with their start and end apart: 5, of which 5 were waited for; matrix products, arithmetic and copies ran while one was open for 6% of the time, Pallas kernels for 0%

profile of v1, /device:TPU:2, one launch (start us, length us, event | category | flops | bytes accessed | tf_op | source)
XLA Modules:
  0.0 403.0 jit_solution(16762831641831608389)
XLA Ops:
  6.7 3.6 gather_fusion.1
  11.8 10.2 %all-to-all-start = ((bf16[32,1,10]{2,1,0:T(2,128)(2,1)}), bf16[32,1,10]{2,1,0:T(2,128)(2,1)S(1)}, u32[]{:S(2)}, u32[]{:S(2)}) async-start(bf16[32,1,10]{2,1,0:T(2,128)(2,1)} %copy.24), calls=%async_computation | async-start | bytes 32768 | tf_op jit(solution)/shard_map/all_to_all | solution.py:167
  26.3 4.3 %all-to-all-done = bf16[32,1,10]{2,1,0:T(2,128)(2,1)S(1)} async-done(((bf16[32,1,10]{2,1,0:T(2,128)(2,1)}), bf16[32,1,10]{2,1,0:T(2,128)(2,1)S(1)}, u32[]{:S(2)}, u32[]{:S(2)}) %all-to-all-start) | async-done | bytes 672 | tf_op jit(solution)/shard_map/all_to_all | solution.py:167
  30.6 5.5 %all-to-all-start.1 = ((bf16[32,10,1024]{2,1,0:T(8,128)(2,1)}), bf16[32,10,1024]{2,1,0:T(8,128)(2,1)}, u32[]{:S(2)}, u32[]{:S(2)}) async-start(bf16[32,10,1024]{2,1,0:T(8,128)(2,1)} %select_select_fusion.3), calls=%async_computation.1 | async-start | bytes 2097152 | tf_op jit(solution)/shard_map/all_to_all | solution.py:166
  36.2 3.0 gather_fusion.5
  43.2 20.5 %all-to-all-done.1 = bf16[32,10,1024]{2,1,0:T(8,128)(2,1)} async-done(((bf16[32,10,1024]{2,1,0:T(8,128)(2,1)}), bf16[32,10,1024]{2,1,0:T(8,128)(2,1)}, u32[]{:S(2)}, u32[]{:S(2)}) %all-to-all-start.1) | async-done | bytes 655392 | tf_op jit(solution)/shard_map/all_to_all | solution.py:166
  63.7 5.6 %all-to-all-start.3 = ((bf16[32,10,2048]{2,1,0:T(8,128)(2,1)}), bf16[32,10,2048]{2,1,0:T(8,128)(2,1)S(1)}, u32[]{:S(2)}, u32[]{:S(2)}) async-start(bf16[32,10,2048]{2,1,0:T(8,128)(2,1)} %select_select_fusion.1), calls=%async_computation.3 | async-start | bytes 4194304 | tf_op jit(solution)/shard_map/all_to_all | solution.py:165
  74.3 2.8 gather_fusion.4
  78.1 39.7 %all-to-all-done.3 = bf16[32,10,2048]{2,1,0:T(8,128)(2,1)S(1)} async-done(((bf16[32,10,2048]{2,1,0:T(8,128)(2,1)}), bf16[32,10,2048]{2,1,0:T(8,128)(2,1)S(1)}, u32[]{:S(2)}, u32[]{:S(2)}) %all-to-all-start.3) | async-done | bytes 1310752 | tf_op jit(solution)/shard_map/all_to_all | solution.py:165
  117.8 3.5 stack.2
  121.2 6.4 %all-to-all-start.2 = ((bf16[32,96,1024]{2,1,0:T(8,128)(2,1)}), bf16[32,96,1024]{2,1,0:T(8,128)(2,1)}, u32[]{:S(2)}, u32[]{:S(2)}) async-start(bf16[32,96,1024]{2,1,0:T(8,128)(2,1)} %stack.2), calls=%async_computation.2 | async-start | bytes 12582912 | tf_op jit(solution)/shard_map/all_to_all | solution.py:19
  128.0 2.5 reshape.585
  132.5 135.0 %all-to-all-done.2 = bf16[32,96,1024]{2,1,0:T(8,128)(2,1)} async-done(((bf16[32,96,1024]{2,1,0:T(8,128)(2,1)}), bf16[32,96,1024]{2,1,0:T(8,128)(2,1)}, u32[]{:S(2)}, u32[]{:S(2)}) %all-to-all-start.2) | async-done | bytes 6291488 | tf_op jit(solution)/shard_map/all_to_all | solution.py:19
  267.5 64.0 %while.17 = (s32[]{:T(128)}, f32[4,4,96]{2,1,0:T(4,128)S(1)}, f32[4,4,96]{2,1,0:T(4,128)S(1)}, f32[96,4,4,128]{3,0,2,1:T(8,128)}, s32[6]{0:T(128)S(1)}, /*index=...) while((s32[]{:T(128)}, f32[4,4,96]{2,1,0:T(4,128)S(1)}, ...), condition=%wide.region_5.6_spmd.clone, body=%wide.region_2.5_spmd.clone.sunk | while | flops 413532864 | bytes 39490572 | solution.py:141
  274.1 2.9 fusion.85
  284.8 2.9 fusion.85
  295.5 2.9 fusion.85
  306.1 2.9 fusion.85
  316.8 2.9 fusion.85
  327.5 2.9 fusion.85
  333.9 3.0 gather_fusion.7
  340.9 4.6 %all-to-all-start.4 = ((bf16[32,10,2048]{2,1,0:T(8,128)(2,1)}), bf16[32,10,2048]{2,1,0:T(8,128)(2,1)}, u32[]{:S(2)}, u32[]{:S(2)}) async-start(bf16[32,10,2048]{2,1,0:T(8,128)(2,1)} %select_select_fusion), calls=%async_computation.4 | async-start | bytes 4194304 | tf_op jit(solution)/shard_map/all_to_all | solution.py:174
  346.9 48.1 %all-to-all-done.4 = bf16[32,10,2048]{2,1,0:T(8,128)(2,1)} async-done(((bf16[32,10,2048]{2,1,0:T(8,128)(2,1)}), bf16[32,10,2048]{2,1,0:T(8,128)(2,1)}, u32[]{:S(2)}, u32[]{:S(2)}) %all-to-all-start.4) | async-done | bytes 1310752 | tf_op jit(solution)/shard_map/all_to_all | solution.py:174
  397.6 3.0 gather_fusion.8
  (181 shorter events, 75.1 us)
Async XLA Ops:
  0.0 36.2 %copy-start = (bf16[288,2048]{1,0:T(8,128)(2,1)S(1)}, bf16[288,2048]{1,0:T(8,128)(2,1)}, u32[]{:S(2)}) copy-start(bf16[288,2048]{1,0:T(8,128)(2,1)} %param.7) | copy-start | bytes 3538948
  0.0 22.8 %copy-start.2 = (bf16[288,1024]{1,0:T(8,128)(2,1)S(1)}, bf16[288,1024]{1,0:T(8,128)(2,1)}, u32[]{:S(2)}) copy-start(bf16[288,1024]{1,0:T(8,128)(2,1)} %param.8) | copy-start | bytes 1769476
  11.8 18.8 %all-to-all-start = ((bf16[32,1,10]{2,1,0:T(2,128)(2,1)}), bf16[32,1,10]{2,1,0:T(2,128)(2,1)S(1)}, u32[]{:S(2)}, u32[]{:S(2)}) async-start(bf16[32,1,10]{2,1,0:T(2,128)(2,1)} %copy.24), calls=%async_computation | async-start | bytes 32768 | tf_op jit(solution)/shard_map/all_to_all | solution.py:167
  30.6 33.1 %all-to-all-start.1 = ((bf16[32,10,1024]{2,1,0:T(8,128)(2,1)}), bf16[32,10,1024]{2,1,0:T(8,128)(2,1)}, u32[]{:S(2)}, u32[]{:S(2)}) async-start(bf16[32,10,1024]{2,1,0:T(8,128)(2,1)} %select_select_fusion.3), calls=%async_computation.1 | async-start | bytes 2097152 | tf_op jit(solution)/shard_map/all_to_all | solution.py:166
  63.7 54.0 %all-to-all-start.3 = ((bf16[32,10,2048]{2,1,0:T(8,128)(2,1)}), bf16[32,10,2048]{2,1,0:T(8,128)(2,1)S(1)}, u32[]{:S(2)}, u32[]{:S(2)}) async-start(bf16[32,10,2048]{2,1,0:T(8,128)(2,1)} %select_select_fusion.1), calls=%async_computation.3 | async-start | bytes 4194304 | tf_op jit(solution)/shard_map/all_to_all | solution.py:165
  117.8 3.5 copy-start.4
  121.2 146.3 %all-to-all-start.2 = ((bf16[32,96,1024]{2,1,0:T(8,128)(2,1)}), bf16[32,96,1024]{2,1,0:T(8,128)(2,1)}, u32[]{:S(2)}, u32[]{:S(2)}) async-start(bf16[32,96,1024]{2,1,0:T(8,128)(2,1)} %stack.2), calls=%async_computation.2 | async-start | bytes 12582912 | tf_op jit(solution)/shard_map/all_to_all | solution.py:19
  270.8 3.2 copy-start.5
  274.1 2.9 copy-start.1
  277.0 1.1 copy-start.6
  281.5 3.2 copy-start.5
  284.8 2.9 copy-start.1
  292.2 3.2 copy-start.5
  295.4 2.9 copy-start.1
  298.4 1.1 copy-start.6
  302.9 3.2 copy-start.5
  306.1 2.9 copy-start.1
  309.1 1.1 copy-start.6
  313.5 3.2 copy-start.5
  316.8 2.9 copy-start.1
  319.7 1.1 copy-start.6
  324.2 3.2 copy-start.5
  327.5 2.9 copy-start.1
  340.9 54.2 %all-to-all-start.4 = ((bf16[32,10,2048]{2,1,0:T(8,128)(2,1)}), bf16[32,10,2048]{2,1,0:T(8,128)(2,1)}, u32[]{:S(2)}, u32[]{:S(2)}) async-start(bf16[32,10,2048]{2,1,0:T(8,128)(2,1)} %select_select_fusion), calls=%async_computation.4 | async-start | bytes 4194304 | tf_op jit(solution)/shard_map/all_to_all | solution.py:174
  (8 other events, 8.3 us)
